TPU v7x, 512 devices: a whole 4x8x8 slice. The times are simulated.
512 devices in a mesh: seq: 64 (over z, y), head: 8 (over x, core).
Axes of the slice: x: 4, y: 8, z: 8, core: 2. Of those that a mesh axis runs over, the one named last changes fastest.
Arguments:
- queries: bfloat16 [2, 4096, 8192], P(None, 'seq', 'head'), may hold values from -10 to 10
- key_states: bfloat16 [2, 4096, 1024], P(None, ('seq', 'head')), may hold values from -10 to 10
- value_state_rows: bfloat16 [2, 4096, 1024], P(None, ('seq', 'head')), may hold values from -6 to 6
- grad_out: bfloat16 [2, 4096, 8192], P(None, 'seq', 'head'), may hold values from -6 to 6
- layouts: int32 [4, 128, 8], replicated, may hold values from 0 to 127, as said below
- plant_ids: int32 [128], replicated, may hold values from 0 to 3
Outputs:
- attended: bfloat16 [2, 4096, 8192], P(None, 'seq', 'head')
- query_grad: bfloat16 [2, 4096, 8192], P(None, 'seq', 'head')
- key_grad: bfloat16 [2, 4096, 1024], P(None, ('seq', 'head'))
- value_grad: bfloat16 [2, 4096, 1024], P(None, ('seq', 'head'))
Inputs may be any that keep to these rules, and one draw needn't show every extreme that they name: Entry 0 of layouts[p, q] is q and every entry is at most q. With owner(b) = b for b < 64 and 127 - b otherwise: if an entry b of layouts[p, q] has owner(b) = o other than owner(q) = d, then b = o when o < d and b = 127 - o when o > d.
All inputs are finite; a program needn't handle non-finite values.
Results may differ from a plain program's by a relative error of at most 0.011.
Values may be sent and summed in bfloat16 or wider, within the bound.
No kernel may reach another device: no remote copies, remote signals or barrier semaphores. Data moves between devices by JAX's collectives and lax.ppermute only.
A program may use at most 64 MiB of HBM per device.

v0:
```python
import jax
import jax.numpy as jnp
from jax import lax
from jax.sharding import PartitionSpec as P

HEAD_SIZE = 128
BLOCK_TOKENS_N = 64
KEY_LIST_SIZE = 8


def live_entries(listed_blocks):
    same_block = listed_blocks[:, None] == listed_blocks[None, :]
    ordinal = jnp.arange(listed_blocks.shape[0], dtype=jnp.int32)
    earlier = ordinal[None, :] < ordinal[:, None]
    return jnp.logical_not(jnp.any(same_block & earlier, axis=1))


def allowed_mask(listed_blocks, live_entry, qblock):
    offsets = jnp.arange(BLOCK_TOKENS_N, dtype=jnp.int32)
    causal = offsets[None, :] <= offsets[:, None]
    diagonal = listed_blocks == qblock
    allowed = live_entry[:, None, None] & (jnp.logical_not(diagonal)[:, None, None] | causal[None])
    return jnp.transpose(allowed, (1, 0, 2)).reshape(BLOCK_TOKENS_N, KEY_LIST_SIZE * BLOCK_TOKENS_N)


def attend_block(query_row_values, gradient_rows, keys_sel, values_sel, allowed, scaling):
    kv_heads = keys_sel.shape[2] // HEAD_SIZE
    head_groups = query_row_values.shape[1] // (kv_heads * HEAD_SIZE)
    query_head_rows = query_row_values.reshape(BLOCK_TOKENS_N, kv_heads, head_groups, HEAD_SIZE)
    gradient_heads = gradient_rows.reshape(BLOCK_TOKENS_N, kv_heads, head_groups, HEAD_SIZE)
    key_head_rows = keys_sel.reshape(KEY_LIST_SIZE * BLOCK_TOKENS_N, kv_heads, HEAD_SIZE)
    value_head_rows = values_sel.reshape(KEY_LIST_SIZE * BLOCK_TOKENS_N, kv_heads, HEAD_SIZE)
    scores = (
        jnp.einsum(
            "qhgd,khd->hgqk", query_head_rows, key_head_rows, preferred_element_type=jnp.float32
        )
        * scaling
    )
    scores = jnp.where(allowed[None, None], scores, -1e30)
    row_max = jnp.max(scores, axis=-1, keepdims=True)
    exponent = jnp.exp(scores - row_max)
    normed = exponent / jnp.sum(exponent, axis=-1, keepdims=True)
    weights = normed.astype(jnp.bfloat16)
    block_out = jnp.einsum(
        "hgqk,khd->qhgd", weights, value_head_rows, preferred_element_type=jnp.float32
    )
    block_out = block_out.astype(jnp.bfloat16).reshape(BLOCK_TOKENS_N, -1)
    grad_probs = jnp.einsum(
        "qhgd,khd->hgqk", gradient_heads, value_head_rows, preferred_element_type=jnp.float32
    )
    row_delta = jnp.sum(normed * grad_probs, axis=-1, keepdims=True)
    grad_scores = (normed * (grad_probs - row_delta)).astype(jnp.bfloat16)
    block_dq = (
        jnp.einsum("hgqk,khd->qhgd", grad_scores, key_head_rows, preferred_element_type=jnp.float32)
        * scaling
    )
    block_dq = block_dq.astype(jnp.bfloat16).reshape(BLOCK_TOKENS_N, -1)
    key_portion = (
        jnp.einsum(
            "hgqk,qhgd->khd", grad_scores, query_head_rows, preferred_element_type=jnp.float32
        )
        * scaling
    )
    value_portion = jnp.einsum(
        "hgqk,qhgd->khd", weights, gradient_heads, preferred_element_type=jnp.float32
    )
    key_portion = key_portion.reshape(KEY_LIST_SIZE, BLOCK_TOKENS_N, kv_heads * HEAD_SIZE)
    value_portion = value_portion.reshape(KEY_LIST_SIZE, BLOCK_TOKENS_N, kv_heads * HEAD_SIZE)
    return (block_out, block_dq, key_portion, value_portion)


def body(queries, key_states, value_state_rows, grad_out, layouts, plant_ids):
    scaling = HEAD_SIZE ** (-0.5)
    seq_count = lax.axis_size("seq")
    device = lax.axis_index("seq")
    count_of_blocks = layouts.shape[1]
    halfway = count_of_blocks // 2
    mine_keys, mine_values = (
        lax.all_to_all(key_states, "head", split_axis=2, concat_axis=1, tiled=True),
        lax.all_to_all(value_state_rows, "head", split_axis=2, concat_axis=1, tiled=True),
    )
    qblocks = jnp.stack([device, count_of_blocks - 1 - device])
    pick_block = jnp.arange(count_of_blocks, dtype=jnp.int32)[None, :] == qblocks[:, None]
    plant_of = jnp.sum(jnp.where(pick_block, plant_ids[None, :], 0), axis=1)
    pick_plant = jnp.arange(layouts.shape[0], dtype=jnp.int32)[None, :] == plant_of[:, None]
    picked = pick_plant[:, :, None, None] & pick_block[:, None, :, None]
    listed_all = jnp.sum(jnp.where(picked, layouts[None], 0), axis=(1, 2))
    owners = jnp.where(listed_all < halfway, listed_all, count_of_blocks - 1 - listed_all)
    upper_half = (listed_all >= halfway).astype(jnp.int32)
    slot_of = jnp.where(owners == device, seq_count + upper_half, owners)
    pool_keys, pool_values = (
        lax.all_gather(mine_keys, "seq", axis=0, tiled=True),
        lax.all_gather(mine_values, "seq", axis=0, tiled=True),
    )
    pool_index = 2 * owners + upper_half
    width = mine_keys.shape[2]
    key_buffer = jnp.zeros((seq_count + 2, BLOCK_TOKENS_N, width), jnp.float32)
    value_buffer = jnp.zeros((seq_count + 2, BLOCK_TOKENS_N, width), jnp.float32)
    slot_ids = jnp.arange(seq_count + 2, dtype=jnp.int32)
    outputs = []
    query_grads = []
    for which_half in range(2):
        listed_blocks = listed_all[which_half]
        live_entry = live_entries(listed_blocks)
        allowed = allowed_mask(listed_blocks, live_entry, qblocks[which_half])
        chosen_index = pool_index[which_half]
        block_out, block_dq, key_portion, value_portion = attend_block(
            queries[which_half],
            grad_out[which_half],
            pool_keys[chosen_index],
            pool_values[chosen_index],
            allowed,
            scaling,
        )
        outputs.append(block_out)
        query_grads.append(block_dq)
        routing = (
            (slot_ids[:, None] == slot_of[which_half][None, :]) & live_entry[None, :]
        ).astype(jnp.float32)
        key_buffer = key_buffer + jnp.einsum(
            "sj,jbf->sbf", routing, key_portion, precision=lax.Precision.HIGHEST
        )
        value_buffer = value_buffer + jnp.einsum(
            "sj,jbf->sbf", routing, value_portion, precision=lax.Precision.HIGHEST
        )
    back_keys, back_values = (
        lax.all_to_all(
            key_buffer[:seq_count].astype(jnp.bfloat16),
            "seq",
            split_axis=0,
            concat_axis=0,
            tiled=True,
        ).astype(jnp.float32),
        lax.all_to_all(
            value_buffer[:seq_count].astype(jnp.bfloat16),
            "seq",
            split_axis=0,
            concat_axis=0,
            tiled=True,
        ).astype(jnp.float32),
    )
    from_higher = (jnp.arange(seq_count, dtype=jnp.int32) > device).astype(jnp.float32)[
        :, None, None
    ]
    from_lower = 1.0 - from_higher
    lower_key = key_buffer[seq_count] + jnp.sum(back_keys * from_higher, axis=0)
    upper_key = key_buffer[seq_count + 1] + jnp.sum(back_keys * from_lower, axis=0)
    lower_value = value_buffer[seq_count] + jnp.sum(back_values * from_higher, axis=0)
    upper_value = value_buffer[seq_count + 1] + jnp.sum(back_values * from_lower, axis=0)
    key_total = jnp.stack([lower_key, upper_key]).astype(jnp.bfloat16)
    value_total = jnp.stack([lower_value, upper_value]).astype(jnp.bfloat16)
    key_grad, value_grad = (
        lax.all_to_all(key_total, "head", split_axis=1, concat_axis=2, tiled=True),
        lax.all_to_all(value_total, "head", split_axis=1, concat_axis=2, tiled=True),
    )
    return (jnp.stack(outputs), jnp.stack(query_grads), key_grad, value_grad)


def solution(mesh):
    in_specs = (
        P(None, "seq", "head"),
        P(None, ("seq", "head"), None),
        P(None, ("seq", "head"), None),
        P(None, "seq", "head"),
        P(),
        P(),
    )
    out_specs = (
        P(None, "seq", "head"),
        P(None, "seq", "head"),
        P(None, ("seq", "head"), None),
        P(None, ("seq", "head"), None),
    )
    return jax.shard_map(body, mesh=mesh, in_specs=in_specs, out_specs=out_specs, check_vma=False)
```

profile of v0, /device:TPU:1, one launch (start us, length us, event | category | flops | bytes accessed | tf_op | source)
XLA Modules:
  0.0 306.1 jit_solution(1030200950925951874)
XLA Ops:
  8.9 13.9 %all_to_all.82 = bf16[8,2,1024]{2,1,0:T(2,128)(2,1)S(1)} all-to-all(bf16[8,2,1024]{2,1,0:T(2,128)(2,1)S(1)} %reshape.429), channel_id=1, replica_groups=mesh['seq'=64,'head'=8] {'head'}, dimensions={0} | all-to-all | bytes 65536 | tf_op jit(solution)/shard_map/all_to_all | solution.py:79
  25.4 7.8 %all_to_all.83 = bf16[8,2,1024]{2,1,0:T(2,128)(2,1)S(1)} all-to-all(bf16[8,2,1024]{2,1,0:T(2,128)(2,1)S(1)} %reshape.427), channel_id=1, replica_groups=mesh['seq'=64,'head'=8] {'head'}, dimensions={0} | all-to-all | bytes 65536 | tf_op jit(solution)/shard_map/all_to_all | solution.py:80
  36.9 66.1 %all-gather.5.cloned.1.call-done = bf16[128,64,128]{2,1,0:T(8,128)(2,1)} async-done(((bf16[2,64,128]{2,1,0:T(8,128)(2,1)}), bf16[128,64,128]{2,1,0:T(8,128)(2,1)}) %all-gather.5.cloned.1.call-update) | async-done | bytes 2097168 | tf_op jit(solution)/shard_map/all_gather | solution.py:92
  103.0 2.2 gather_fusion.3
  105.9 81.0 %all-gather.3.cloned.1.call-done = bf16[128,64,128]{2,1,0:T(8,128)(2,1)} async-done(((bf16[2,64,128]{2,1,0:T(8,128)(2,1)}), bf16[128,64,128]{2,1,0:T(8,128)(2,1)}) %all-gather.3.cloned.1.call-update) | async-done | bytes 2097168 | tf_op jit(solution)/shard_map/all_gather | solution.py:93
  186.9 2.2 gather_fusion.2
  191.9 2.2 gather_fusion.1
  194.8 2.2 gather_fusion
  201.3 1.4 copy-done
  203.0 1.7 copy.77
  204.7 8.7 %all-to-all-start.2 = ((bf16[64,64,128]{2,1,0:T(8,128)(2,1)}), bf16[64,64,128]{2,1,0:T(8,128)(2,1)S(1)}, u32[]{:S(2)}, u32[]{:S(2)}) async-start(bf16[64,64,128]{2,1,0:T(8,128)(2,1)} %copy.77), calls=%async_computation.2 | async-start | bytes 2097152 | tf_op jit(solution)/shard_map/all_to_all | solution.py:127
  213.4 1.5 fusion.22
  218.1 1.4 copy-done.1
  219.8 1.6 copy.83
  221.5 15.4 %all-to-all-done.2 = bf16[64,64,128]{2,1,0:T(8,128)(2,1)S(1)} async-done(((bf16[64,64,128]{2,1,0:T(8,128)(2,1)}), bf16[64,64,128]{2,1,0:T(8,128)(2,1)S(1)}, u32[]{:S(2)}, u32[]{:S(2)}) %all-to-all-start.2) | async-done | bytes 1048608 | tf_op jit(solution)/shard_map/all_to_all | solution.py:127
  236.8 9.9 %all-to-all-start.4 = ((bf16[64,64,128]{2,1,0:T(8,128)(2,1)}), bf16[64,64,128]{2,1,0:T(8,128)(2,1)}, u32[]{:S(2)}, u32[]{:S(2)}) async-start(bf16[64,64,128]{2,1,0:T(8,128)(2,1)} %copy.83), calls=%async_computation.4 | async-start | bytes 2097152 | tf_op jit(solution)/shard_map/all_to_all | solution.py:134
  248.3 1.3 fusion.14
  249.8 1.3 fusion.12
  252.5 19.4 %all-to-all-done.4 = bf16[64,64,128]{2,1,0:T(8,128)(2,1)} async-done(((bf16[64,64,128]{2,1,0:T(8,128)(2,1)}), bf16[64,64,128]{2,1,0:T(8,128)(2,1)}, u32[]{:S(2)}, u32[]{:S(2)}) %all-to-all-start.4) | async-done | bytes 1048608 | tf_op jit(solution)/shard_map/all_to_all | solution.py:134
  271.9 2.0 fusion
  275.8 9.5 %all-to-all-start.3 = ((bf16[2,64,128]{2,0,1:T(2,128)(2,1)}), bf16[2,64,128]{2,0,1:T(2,128)(2,1)S(1)}, u32[]{:S(2)}, u32[]{:S(2)}) async-start(bf16[2,64,128]{2,0,1:T(2,128)(2,1)} %pad_maximum_fusion.2), calls=%async_computation.3 | async-start | bytes 65536 | tf_op jit(solution)/shard_map/all_to_all | solution.py:153
  287.0 2.9 all-to-all-done.3
  289.9 4.0 %all-to-all-start.5 = ((bf16[2,64,128]{2,0,1:T(2,128)(2,1)}), bf16[2,64,128]{2,0,1:T(2,128)(2,1)S(1)}, u32[]{:S(2)}, u32[]{:S(2)}) async-start(bf16[2,64,128]{2,0,1:T(2,128)(2,1)} %pad_maximum_fusion.3), calls=%async_computation.5 | async-start | bytes 65536 | tf_op jit(solution)/shard_map/all_to_all | solution.py:154
  295.2 3.4 %all-to-all-done.5 = bf16[2,64,128]{2,0,1:T(2,128)(2,1)S(1)} async-done(((bf16[2,64,128]{2,0,1:T(2,128)(2,1)}), bf16[2,64,128]{2,0,1:T(2,128)(2,1)S(1)}, u32[]{:S(2)}, u32[]{:S(2)}) %all-to-all-start.5) | async-done | bytes 32800 | tf_op jit(solution)/shard_map/all_to_all | solution.py:154
  (134 shorter events, 28.4 us)
Async XLA Ops:
  7.2 17.3 %copy-start.14 = (bf16[2,8,1024]{2,1,0:T(8,128)(2,1)S(1)}, bf16[2,8,1024]{2,1,0:T(8,128)(2,1)}, u32[]{:S(2)}) copy-start(bf16[2,8,1024]{2,1,0:T(8,128)(2,1)} %param.8) | copy-start | bytes 98308
  7.2 27.7 %copy-start.26 = (s32[128]{0:T(128)S(1)}, s32[128]{0:T(128)}, u32[]{:S(2)}) copy-start(s32[128]{0:T(128)} %param.11) | copy-start | bytes 1540
  7.2 28.1 %copy-start.15 = (s32[4,128,8]{1,2,0:T(8,128)S(1)}, s32[4,128,8]{1,2,0:T(8,128)}, u32[]{:S(2)}) copy-start(s32[4,128,8]{1,2,0:T(8,128)} %param.10) | copy-start | bytes 49156
  7.2 29.3 %copy-start.5 = (bf16[2,64,1024]{2,1,0:T(8,128)(2,1)S(1)}, bf16[2,64,1024]{2,1,0:T(8,128)(2,1)}, u32[]{:S(2)}) copy-start(bf16[2,64,1024]{2,1,0:T(8,128)(2,1)} %param.6) | copy-start | bytes 786436
  7.2 95.8 %all-gather.5.cloned.1.call-start = ((), (), s32[]{:S(2)}) async-start(), calls=%async_computation.7 | async-start | bytes 2129920 | tf_op jit(solution)/shard_map/all_gather | solution.py:92
  22.8 13.8 %copy-start.6 = (bf16[2,64,1024]{2,1,0:T(8,128)(2,1)S(1)}, bf16[2,64,1024]{2,1,0:T(8,128)(2,1)}, u32[]{:S(2)}) copy-start(bf16[2,64,1024]{2,1,0:T(8,128)(2,1)} %param.9) | copy-start | bytes 786436
  24.4 162.5 %all-gather.3.cloned.1.call-start = ((), (), s32[]{:S(2)}) async-start(), calls=%async_computation.6 | async-start | bytes 2129920 | tf_op jit(solution)/shard_map/all_gather | solution.py:93
  36.0 162.8 %copy-start.20 = (pred[8]{0:T(512)(128)(4,1)}, pred[8]{0:T(512)(128)(4,1)S(1)}, u32[]{:S(2)}) copy-start(pred[8]{0:T(512)(128)(4,1)S(1)} %not.36) | copy-start | bytes 28
  36.0 164.0 %copy-start.22 = (pred[8]{0:T(512)(128)(4,1)}, pred[8]{0:T(512)(128)(4,1)S(1)}, u32[]{:S(2)}) copy-start(pred[8]{0:T(512)(128)(4,1)S(1)} %not.38) | copy-start | bytes 28
  36.7 160.3 %copy-start.8 = (bf16[8,8,8,128]{3,2,1,0:T(8,128)(2,1)}, bf16[8,8,8,128]{3,2,1,0:T(8,128)(2,1)S(1)}, u32[]{:S(2)}) copy-start(bf16[8,8,8,128]{3,2,1,0:T(8,128)(2,1)S(1)} %copy.87) | copy-start | bytes 393220
  36.7 152.7 %copy-start.10 = (bf16[8,8,8,128]{3,2,1,0:T(8,128)(2,1)}, bf16[8,8,8,128]{3,2,1,0:T(8,128)(2,1)S(1)}, u32[]{:S(2)}) copy-start(bf16[8,8,8,128]{3,2,1,0:T(8,128)(2,1)S(1)} %copy.88) | copy-start | bytes 393220
  36.8 162.0 %copy-start.16 = (s32[8]{0:T(128)}, s32[8]{0:T(128)S(1)}, u32[]{:S(2)}) copy-start(s32[8]{0:T(128)S(1)} %get-tuple-element.21) | copy-start | bytes 100
  36.8 163.2 %copy-start.18 = (s32[8]{0:T(128)}, s32[8]{0:T(128)S(1)}, u32[]{:S(2)}) copy-start(s32[8]{0:T(128)S(1)} %get-tuple-element.20) | copy-start | bytes 100
  198.0 2.0 copy-start.7
  201.3 1.4 copy-start
  204.7 32.1 %all-to-all-start.2 = ((bf16[64,64,128]{2,1,0:T(8,128)(2,1)}), bf16[64,64,128]{2,1,0:T(8,128)(2,1)S(1)}, u32[]{:S(2)}, u32[]{:S(2)}) async-start(bf16[64,64,128]{2,1,0:T(8,128)(2,1)} %copy.77), calls=%async_computation.2 | async-start | bytes 2097152 | tf_op jit(solution)/shard_map/all_to_all | solution.py:127
  213.4 1.5 copy-start.9
  219.8 27.9 %copy-start.12 = (bf16[8,64,128]{2,1,0:T(8,128)(2,1)S(1)}, bf16[8,64,128]{2,1,0:T(8,128)(2,1)}, u32[]{:S(2)}) copy-start(bf16[8,64,128]{2,1,0:T(8,128)(2,1)} %copy-done.11) | copy-start | bytes 393220
  236.8 35.1 %all-to-all-start.4 = ((bf16[64,64,128]{2,1,0:T(8,128)(2,1)}), bf16[64,64,128]{2,1,0:T(8,128)(2,1)}, u32[]{:S(2)}, u32[]{:S(2)}) async-start(bf16[64,64,128]{2,1,0:T(8,128)(2,1)} %copy.83), calls=%async_computation.4 | async-start | bytes 2097152 | tf_op jit(solution)/shard_map/all_to_all | solution.py:134
  249.8 1.5 copy-start.4
  249.8 22.1 %copy-start.24 = (f32[64]{0:T(128)S(1)}, f32[64]{0:T(128)}, u32[]{:S(2)}) copy-start(f32[64]{0:T(128)} %broadcast_subtract_fusion) | copy-start | bytes 772
  249.8 22.1 %copy-start.25 = (f32[64]{0:T(128)S(1)}, f32[64]{0:T(128)}, u32[]{:S(2)}) copy-start(f32[64]{0:T(128)} %compare_convert_fusion) | copy-start | bytes 772
  275.8 14.2 %all-to-all-start.3 = ((bf16[2,64,128]{2,0,1:T(2,128)(2,1)}), bf16[2,64,128]{2,0,1:T(2,128)(2,1)S(1)}, u32[]{:S(2)}, u32[]{:S(2)}) async-start(bf16[2,64,128]{2,0,1:T(2,128)(2,1)} %pad_maximum_fusion.2), calls=%async_computation.3 | async-start | bytes 65536 | tf_op jit(solution)/shard_map/all_to_all | solution.py:153
  289.9 8.7 %all-to-all-start.5 = ((bf16[2,64,128]{2,0,1:T(2,128)(2,1)}), bf16[2,64,128]{2,0,1:T(2,128)(2,1)S(1)}, u32[]{:S(2)}, u32[]{:S(2)}) async-start(bf16[2,64,128]{2,0,1:T(2,128)(2,1)} %pad_maximum_fusion.3), calls=%async_computation.5 | async-start | bytes 65536 | tf_op jit(solution)/shard_map/all_to_all | solution.py:154
  (9 other events, 8.3 us)
Sparse Core Ops, SparseCore 0:
  24.5 78.4 all-gather.4
  106.6 80.2 all-gather.2
where the time goes:
time: 307 us; the launch traced here: 306 us
  waiting for transfers between devices  188 us (61%)
  starting transfers between devices  32.1 us (10%)
  local copies, waits for them, and re-layouts  25.6 us (8%)
  blocking collectives  21.7 us (7%)
  between operations  14.8 us (5%)
  matrix products  13.3 us (4%)
  other arithmetic  10.4 us (3%)
    all_gather x1, waiting for transfers between devices, body(): lax.all_gather(mine_values, 'seq', axis=0, tiled=True)  81 us
    all_gather x1, waiting for transfers between devices, body(): lax.all_gather(mine_keys, 'seq', axis=0, tiled=True)  66.1 us
    all_to_all x1, waiting for transfers between devices, body(): lax.all_to_all(value_buffer[:seq_count].astype(jnp.bfloat16), 'seq', spli...  19.4 us
    all_to_all x1, waiting for transfers between devices, body(): lax.all_to_all(key_buffer[:seq_count].astype(jnp.bfloat16), 'seq', split_...  15.4 us
    all_to_all x1, blocking collectives, body(): lax.all_to_all(key_states, 'head', split_axis=2, concat_axis=1, tiled=True)  13.9 us
    all_to_all x1, starting transfers between devices, body(): lax.all_to_all(value_buffer[:seq_count].astype(jnp.bfloat16), 'seq', spli...  9.89 us
    all_to_all x1, starting transfers between devices, body(): lax.all_to_all(key_total, 'head', split_axis=1, concat_axis=2, tiled=True)  9.46 us
    all_to_all x1, starting transfers between devices, body(): lax.all_to_all(key_buffer[:seq_count].astype(jnp.bfloat16), 'seq', split_...  8.74 us
  transfers between devices with their start and end apart: 6, of which 6 were waited for; matrix products, arithmetic and copies ran while one was open for 7% of the time, Pallas kernels for 0%

commit v1 on v0

--- a/solution.py
+++ b/solution.py
@@ -75,9 +75,21 @@
     device = lax.axis_index("seq")
     count_of_blocks = layouts.shape[1]
     halfway = count_of_blocks // 2
+
+    def cards_launch(block_here):
+        return jnp.concatenate(
+            lax.all_to_all(
+                jnp.stack(jnp.split(block_here, lax.axis_size("head"), axis=2)),
+                axis_name="head",
+                split_axis=0,
+                concat_axis=0,
+            ),
+            axis=1,
+        )
+
     mine_keys, mine_values = (
         lax.all_to_all(key_states, "head", split_axis=2, concat_axis=1, tiled=True),
-        lax.all_to_all(value_state_rows, "head", split_axis=2, concat_axis=1, tiled=True),
+        cards_launch(value_state_rows),
     )
     qblocks = jnp.stack([device, count_of_blocks - 1 - device])
     pick_block = jnp.arange(count_of_blocks, dtype=jnp.int32)[None, :] == qblocks[:, None]

time: 307 us -> 307 us (level)
    unnamed x66 -> x70, local copies, waits for them, and re-layouts: 8.57 us -> 9.19 us
where the time goes in v1:
time: 307 us; the launch traced here: 306 us
  waiting for transfers between devices  188 us (61%)
  starting transfers between devices  32.1 us (10%)
  local copies, waits for them, and re-layouts  25.9 us (8%)
  blocking collectives  21.7 us (7%)
  between operations  14.7 us (5%)
  matrix products  13.2 us (4%)
  other arithmetic  10.4 us (3%)
    all_gather x1, waiting for transfers between devices, body(): lax.all_gather(mine_values, 'seq', axis=0, tiled=True)  81 us
    all_gather x1, waiting for transfers between devices, body(): lax.all_gather(mine_keys, 'seq', axis=0, tiled=True)  65.8 us
    all_to_all x1, waiting for transfers between devices, body(): lax.all_to_all(value_buffer[:seq_count].astype(jnp.bfloat16), 'seq', spli...  19.4 us
    all_to_all x1, waiting for transfers between devices, body(): lax.all_to_all(key_buffer[:seq_count].astype(jnp.bfloat16), 'seq', split_...  15.4 us
    all_to_all x1, blocking collectives, body(): lax.all_to_all(key_states, 'head', split_axis=2, concat_axis=1, tiled=True)  13.9 us
    all_to_all x1, starting transfers between devices, body(): lax.all_to_all(value_buffer[:seq_count].astype(jnp.bfloat16), 'seq', spli...  9.89 us
    all_to_all x1, starting transfers between devices, body(): lax.all_to_all(key_total, 'head', split_axis=1, concat_axis=2, tiled=True)  9.46 us
    unnamed x70, local copies, waits for them, and re-layouts  9.19 us
  transfers between devices with their start and end apart: 6, of which 6 were waited for; matrix products, arithmetic and copies ran while one was open for 7% of the time, Pallas kernels for 0%

profile of v1, /device:TPU:1, one launch (start us, length us, event | category | flops | bytes accessed | tf_op | source)
XLA Modules:
  0.0 306.1 jit_solution(2717361965055213140)
XLA Ops:
  8.9 13.9 %all_to_all.69 = bf16[8,2,1024]{2,1,0:T(2,128)(2,1)S(1)} all-to-all(bf16[8,2,1024]{2,1,0:T(2,128)(2,1)S(1)} %reshape.435), channel_id=1, replica_groups=mesh['seq'=64,'head'=8] {'head'}, dimensions={0} | all-to-all | bytes 65536 | tf_op jit(solution)/shard_map/all_to_all | solution.py:91
  26.6 7.8 %all_to_all.70 = bf16[8,2,8,128]{3,2,1,0:T(8,128)(2,1)S(1)} all-to-all(bf16[8,2,8,128]{3,2,1,0:T(8,128)(2,1)S(1)} %constant_dynamic-update-slice_fusion), channel_id=1, replica_groups=mesh['seq'=64,'head'=8] {'head'}, dimensions={0} | all-to-all | bytes 65536 | tf_op jit(solution)/shard_map/all_to_all | solution.py:81
  37.2 65.8 %all-gather.5.cloned.1.call-done = bf16[128,64,128]{2,1,0:T(8,128)(2,1)} async-done(((bf16[2,64,128]{2,1,0:T(8,128)(2,1)}), bf16[128,64,128]{2,1,0:T(8,128)(2,1)}) %all-gather.5.cloned.1.call-update) | async-done | bytes 2097168 | tf_op jit(solution)/shard_map/all_gather | solution.py:104
  103.0 2.2 gather_fusion.3
  105.9 81.0 %all-gather.3.cloned.1.call-done = bf16[128,64,128]{2,1,0:T(8,128)(2,1)} async-done(((bf16[2,64,128]{2,1,0:T(8,128)(2,1)}), bf16[128,64,128]{2,1,0:T(8,128)(2,1)}) %all-gather.3.cloned.1.call-update) | async-done | bytes 2097168 | tf_op jit(solution)/shard_map/all_gather | solution.py:105
  186.9 2.2 gather_fusion.2
  191.9 2.2 gather_fusion.1
  194.8 2.2 gather_fusion
  201.3 1.4 copy-done
  203.0 1.7 copy.75
  204.7 8.7 %all-to-all-start.2 = ((bf16[64,64,128]{2,1,0:T(8,128)(2,1)}), bf16[64,64,128]{2,1,0:T(8,128)(2,1)S(1)}, u32[]{:S(2)}, u32[]{:S(2)}) async-start(bf16[64,64,128]{2,1,0:T(8,128)(2,1)} %copy.75), calls=%async_computation.2 | async-start | bytes 2097152 | tf_op jit(solution)/shard_map/all_to_all | solution.py:139
  213.5 1.5 fusion.22
  218.1 1.4 copy-done.1
  219.8 1.6 copy.81
  221.5 15.4 %all-to-all-done.2 = bf16[64,64,128]{2,1,0:T(8,128)(2,1)S(1)} async-done(((bf16[64,64,128]{2,1,0:T(8,128)(2,1)}), bf16[64,64,128]{2,1,0:T(8,128)(2,1)S(1)}, u32[]{:S(2)}, u32[]{:S(2)}) %all-to-all-start.2) | async-done | bytes 1048608 | tf_op jit(solution)/shard_map/all_to_all | solution.py:139
  236.8 9.9 %all-to-all-start.4 = ((bf16[64,64,128]{2,1,0:T(8,128)(2,1)}), bf16[64,64,128]{2,1,0:T(8,128)(2,1)}, u32[]{:S(2)}, u32[]{:S(2)}) async-start(bf16[64,64,128]{2,1,0:T(8,128)(2,1)} %copy.81), calls=%async_computation.4 | async-start | bytes 2097152 | tf_op jit(solution)/shard_map/all_to_all | solution.py:146
  248.3 1.3 fusion.14
  249.8 1.3 fusion.12
  252.6 19.4 %all-to-all-done.4 = bf16[64,64,128]{2,1,0:T(8,128)(2,1)} async-done(((bf16[64,64,128]{2,1,0:T(8,128)(2,1)}), bf16[64,64,128]{2,1,0:T(8,128)(2,1)}, u32[]{:S(2)}, u32[]{:S(2)}) %all-to-all-start.4) | async-done | bytes 1048608 | tf_op jit(solution)/shard_map/all_to_all | solution.py:146
  271.9 2.0 fusion
  275.8 9.5 %all-to-all-start.3 = ((bf16[2,64,128]{2,0,1:T(2,128)(2,1)}), bf16[2,64,128]{2,0,1:T(2,128)(2,1)S(1)}, u32[]{:S(2)}, u32[]{:S(2)}) async-start(bf16[2,64,128]{2,0,1:T(2,128)(2,1)} %pad_maximum_fusion.2), calls=%async_computation.3 | async-start | bytes 65536 | tf_op jit(solution)/shard_map/all_to_all | solution.py:165
  287.0 2.9 all-to-all-done.3
  290.0 4.0 %all-to-all-start.5 = ((bf16[2,64,128]{2,0,1:T(2,128)(2,1)}), bf16[2,64,128]{2,0,1:T(2,128)(2,1)S(1)}, u32[]{:S(2)}, u32[]{:S(2)}) async-start(bf16[2,64,128]{2,0,1:T(2,128)(2,1)} %pad_maximum_fusion.3), calls=%async_computation.5 | async-start | bytes 65536 | tf_op jit(solution)/shard_map/all_to_all | solution.py:166
  295.3 3.4 %all-to-all-done.5 = bf16[2,64,128]{2,0,1:T(2,128)(2,1)S(1)} async-done(((bf16[2,64,128]{2,0,1:T(2,128)(2,1)}), bf16[2,64,128]{2,0,1:T(2,128)(2,1)S(1)}, u32[]{:S(2)}, u32[]{:S(2)}) %all-to-all-start.5) | async-done | bytes 32800 | tf_op jit(solution)/shard_map/all_to_all | solution.py:166
  (139 shorter events, 28.7 us)
Async XLA Ops:
  7.2 19.4 %copy-start.14 = (bf16[2,8,1024]{2,1,0:T(8,128)(2,1)S(1)}, bf16[2,8,1024]{2,1,0:T(8,128)(2,1)}, u32[]{:S(2)}) copy-start(bf16[2,8,1024]{2,1,0:T(8,128)(2,1)} %param.8) | copy-start | bytes 98308
  7.2 28.0 %copy-start.26 = (s32[128]{0:T(128)S(1)}, s32[128]{0:T(128)}, u32[]{:S(2)}) copy-start(s32[128]{0:T(128)} %param.11) | copy-start | bytes 1540
  7.2 28.4 %copy-start.15 = (s32[4,128,8]{1,2,0:T(8,128)S(1)}, s32[4,128,8]{1,2,0:T(8,128)}, u32[]{:S(2)}) copy-start(s32[4,128,8]{1,2,0:T(8,128)} %param.10) | copy-start | bytes 49156
  7.2 29.7 %copy-start.5 = (bf16[2,64,1024]{2,1,0:T(8,128)(2,1)S(1)}, bf16[2,64,1024]{2,1,0:T(8,128)(2,1)}, u32[]{:S(2)}) copy-start(bf16[2,64,1024]{2,1,0:T(8,128)(2,1)} %param.6) | copy-start | bytes 786436
  7.2 29.7 %copy-start.6 = (bf16[2,64,1024]{2,1,0:T(8,128)(2,1)S(1)}, bf16[2,64,1024]{2,1,0:T(8,128)(2,1)}, u32[]{:S(2)}) copy-start(bf16[2,64,1024]{2,1,0:T(8,128)(2,1)} %param.9) | copy-start | bytes 786436
  7.2 95.8 %all-gather.5.cloned.1.call-start = ((), (), s32[]{:S(2)}) async-start(), calls=%async_computation.7 | async-start | bytes 2129920 | tf_op jit(solution)/shard_map/all_gather | solution.py:104
  24.4 162.5 %all-gather.3.cloned.1.call-start = ((), (), s32[]{:S(2)}) async-start(), calls=%async_computation.6 | async-start | bytes 2129920 | tf_op jit(solution)/shard_map/all_gather | solution.py:105
  36.3 162.5 %copy-start.20 = (pred[8]{0:T(512)(128)(4,1)}, pred[8]{0:T(512)(128)(4,1)S(1)}, u32[]{:S(2)}) copy-start(pred[8]{0:T(512)(128)(4,1)S(1)} %not.36) | copy-start | bytes 28
  36.3 163.7 %copy-start.22 = (pred[8]{0:T(512)(128)(4,1)}, pred[8]{0:T(512)(128)(4,1)S(1)}, u32[]{:S(2)}) copy-start(pred[8]{0:T(512)(128)(4,1)S(1)} %not.38) | copy-start | bytes 28
  37.0 160.0 %copy-start.8 = (bf16[8,8,8,128]{3,2,1,0:T(8,128)(2,1)}, bf16[8,8,8,128]{3,2,1,0:T(8,128)(2,1)S(1)}, u32[]{:S(2)}) copy-start(bf16[8,8,8,128]{3,2,1,0:T(8,128)(2,1)S(1)} %copy.85) | copy-start | bytes 393220
  37.0 152.5 %copy-start.10 = (bf16[8,8,8,128]{3,2,1,0:T(8,128)(2,1)}, bf16[8,8,8,128]{3,2,1,0:T(8,128)(2,1)S(1)}, u32[]{:S(2)}) copy-start(bf16[8,8,8,128]{3,2,1,0:T(8,128)(2,1)S(1)} %copy.86) | copy-start | bytes 393220
  37.1 161.7 %copy-start.16 = (s32[8]{0:T(128)}, s32[8]{0:T(128)S(1)}, u32[]{:S(2)}) copy-start(s32[8]{0:T(128)S(1)} %get-tuple-element.21) | copy-start | bytes 100
  37.1 162.9 %copy-start.18 = (s32[8]{0:T(128)}, s32[8]{0:T(128)S(1)}, u32[]{:S(2)}) copy-start(s32[8]{0:T(128)S(1)} %get-tuple-element.20) | copy-start | bytes 100
  198.0 2.0 copy-start.7
  201.3 1.4 copy-start
  204.7 32.1 %all-to-all-start.2 = ((bf16[64,64,128]{2,1,0:T(8,128)(2,1)}), bf16[64,64,128]{2,1,0:T(8,128)(2,1)S(1)}, u32[]{:S(2)}, u32[]{:S(2)}) async-start(bf16[64,64,128]{2,1,0:T(8,128)(2,1)} %copy.75), calls=%async_computation.2 | async-start | bytes 2097152 | tf_op jit(solution)/shard_map/all_to_all | solution.py:139
  213.5 1.5 copy-start.9
  219.8 27.9 %copy-start.12 = (bf16[8,64,128]{2,1,0:T(8,128)(2,1)S(1)}, bf16[8,64,128]{2,1,0:T(8,128)(2,1)}, u32[]{:S(2)}) copy-start(bf16[8,64,128]{2,1,0:T(8,128)(2,1)} %copy-done.11) | copy-start | bytes 393220
  236.8 35.1 %all-to-all-start.4 = ((bf16[64,64,128]{2,1,0:T(8,128)(2,1)}), bf16[64,64,128]{2,1,0:T(8,128)(2,1)}, u32[]{:S(2)}, u32[]{:S(2)}) async-start(bf16[64,64,128]{2,1,0:T(8,128)(2,1)} %copy.81), calls=%async_computation.4 | async-start | bytes 2097152 | tf_op jit(solution)/shard_map/all_to_all | solution.py:146
  249.8 1.5 copy-start.4
  249.8 22.1 %copy-start.24 = (f32[64]{0:T(128)S(1)}, f32[64]{0:T(128)}, u32[]{:S(2)}) copy-start(f32[64]{0:T(128)} %broadcast_subtract_fusion) | copy-start | bytes 772
  249.8 22.1 %copy-start.25 = (f32[64]{0:T(128)S(1)}, f32[64]{0:T(128)}, u32[]{:S(2)}) copy-start(f32[64]{0:T(128)} %compare_convert_fusion) | copy-start | bytes 772
  275.8 14.2 %all-to-all-start.3 = ((bf16[2,64,128]{2,0,1:T(2,128)(2,1)}), bf16[2,64,128]{2,0,1:T(2,128)(2,1)S(1)}, u32[]{:S(2)}, u32[]{:S(2)}) async-start(bf16[2,64,128]{2,0,1:T(2,128)(2,1)} %pad_maximum_fusion.2), calls=%async_computation.3 | async-start | bytes 65536 | tf_op jit(solution)/shard_map/all_to_all | solution.py:165
  290.0 8.7 %all-to-all-start.5 = ((bf16[2,64,128]{2,0,1:T(2,128)(2,1)}), bf16[2,64,128]{2,0,1:T(2,128)(2,1)S(1)}, u32[]{:S(2)}, u32[]{:S(2)}) async-start(bf16[2,64,128]{2,0,1:T(2,128)(2,1)} %pad_maximum_fusion.3), calls=%async_computation.5 | async-start | bytes 65536 | tf_op jit(solution)/shard_map/all_to_all | solution.py:166
  (9 other events, 8.2 us)
Sparse Core Ops, SparseCore 0:
  24.5 78.4 all-gather.4
  106.6 80.2 all-gather.2
